TPU v7x, 256 devices: a whole 4x4x8 slice. The times are simulated.
256 devices in a mesh: rows: 64 (over y, z, core), rhs: 4 (over x).
Axes of the slice: x: 4, y: 4, z: 8, core: 2. Of those that a mesh axis runs over, the one named last changes fastest.
Arguments:
- kernel_rows: bfloat16 [131072, 512], P(('rows', 'rhs')), may hold values from 0 to 1
- factor_blocks: bfloat16 [512, 8, 256, 256], P('rows'), may hold values from -0.125 to 0.125
- diag_inverse: bfloat16 [512, 256, 256], P('rows'), as said below
- pattern: int32 [512, 8], P('rows'), may hold values from 0 to 511, as said below
- live_counts: int32 [512], P('rows'), may hold values from 0 to 8, as said below
Outputs:
- solution: bfloat16 [131072, 512], P('rows', 'rhs')
Inputs may be any that keep to these rules, and one draw needn't show every extreme that they name: pattern[s, k] names a block row of a lower level than s; slot 0 of every block row above level 0 names a block row of the level just below; rows of level 0 hold 0. Block row t is held by index t // 8 of rows; the used slots of the block rows held by one index of rows name, for any one level, at most 1 distinct block rows held by any one other index. `live_counts`: 0 on level 0, from 1 to 8 on higher levels, 8 reached. `diag_inverse`: each block is the inverse of a well-conditioned diagonal block of the factor.
All inputs are finite; a program needn't handle non-finite values.
Results may differ from a plain program's by a relative error of at most 0.0058.
Values may be sent and summed in bfloat16 or wider, within the bound.
No kernel may reach another device: no remote copies, remote signals or barrier semaphores. Data moves between devices by JAX's collectives and lax.ppermute only.
A program may use at most 128 MiB of HBM per device.

v0:
```python
import jax
import jax.numpy as jnp
from jax import lax
from jax.sharding import PartitionSpec as P

LEV = 4


def shards(kernel_rows, factor_blocks, diag_inverse, pattern, live_counts):
    received = lax.all_to_all(kernel_rows, "rhs", split_axis=1, concat_axis=0, tiled=True)
    per_device = factor_blocks.shape[0]
    slot_count = factor_blocks.shape[1]
    block = factor_blocks.shape[2]
    width = received.shape[1]
    right_side = received.reshape(per_device, block, width)
    holders = lax.axis_size("rows")
    per_level = per_device // LEV
    level_size = holders * per_level
    level_of = pattern % per_device // per_level
    holder_of = pattern // per_device
    offset_of = pattern % per_level
    active = jnp.arange(slot_count)[None, :] < live_counts[:, None]
    position = holder_of * per_level + offset_of
    flat_index = level_of * level_size + position
    gathered_all = []
    solved_all = []
    for level_now in range(LEV):
        lower = level_now * per_level
        upper = lower + per_level
        if level_now == 0:
            summed_now = jnp.zeros((per_level, block, width), jnp.float32)
        else:
            available = jnp.concatenate(gathered_all, axis=0)
            picked = jnp.take(available, flat_index[lower:upper], axis=0, mode="clip")
            picked = jnp.where(active[lower:upper, :, None, None], picked, jnp.zeros_like(picked))
            summed_now = jnp.einsum(
                "bkij,bkjr->bir",
                factor_blocks[lower:upper],
                picked,
                preferred_element_type=jnp.float32,
            )
        residual = (right_side[lower:upper].astype(jnp.float32) - summed_now).astype(jnp.bfloat16)
        solved = jnp.einsum(
            "bij,bjr->bir", diag_inverse[lower:upper], residual, preferred_element_type=jnp.float32
        ).astype(jnp.bfloat16)
        solved_all.append(solved)
        if level_now + 1 < LEV:
            incoming = lax.all_gather(solved, "rows", axis=0, tiled=True)
            gathered_all.append(incoming)
    return jnp.concatenate(solved_all, axis=0).reshape(per_device * block, width)


def solution(mesh):
    placed = (
        P(("rows", "rhs"), None),
        P("rows", None, None, None),
        P("rows", None, None),
        P("rows", None),
        P("rows"),
    )
    return jax.shard_map(
        shards, mesh=mesh, in_specs=placed, out_specs=P("rows", "rhs"), check_vma=False
    )
```

profile of v0, /device:TPU:1, one launch (start us, length us, event | category | flops | bytes accessed | tf_op | source)
XLA Modules:
  0.0 339.4 jit_solution(18205425547887080133)
XLA Ops:
  6.5 1.3 copy.30
  7.8 13.2 %all_to_all.16 = bf16[512,4,128]{0,2,1:T(8,128)(2,1)S(1)} all-to-all(bf16[512,4,128]{0,2,1:T(8,128)(2,1)S(1)} %bitcast.60), channel_id=1, replica_groups=mesh['rows'=64,'rhs'=4] {'rhs'}, dimensions={1} | all-to-all | bytes 1048576 | tf_op jit(solution)/shard_map/all_to_all | solution.py:10
  21.0 0.1 fusion.84
  21.0 0.1 copy.31
  21.2 1.8 convolution_convert_fusion
  23.0 0.0 all-gather.6.cloned.1.call-start
  23.1 0.7 fusion.71
  23.8 0.1 reshape.28
  23.9 0.7 iota_compare_fusion
  24.6 0.1 copy.32
  24.7 0.1 copy.34
  24.9 84.1 %all-gather.4.cloned.1.call-done = bf16[128,256,128]{2,1,0:T(8,128)(2,1)} async-done(((bf16[2,256,128]{2,1,0:T(8,128)(2,1)}), bf16[128,256,128]{2,1,0:T(8,128)(2,1)}) %all-gather.4.cloned.1.call-update) | async-done | bytes 8388624 | tf_op jit(solution)/shard_map/all_gather | solution.py:48
  109.0 4.1 %gather_fusion = bf16[16,256,128]{2,1,0:T(8,128)(2,1)S(1)} fusion(bf16[128,256,128]{2,1,0:T(8,128)(2,1)} %all-gather.4.cloned.1.call-done, s32[1024]{0:T(1024)S(1)} %pad_clamp_fusion.2), kind=kCustom, calls=%fused_computation | custom fusion | bytes 2097216 | tf_op jit(solution)/shard_map/jit(_take)/gather | solution.py:34
  113.1 0.5 copy.33
  113.7 3.3 fusion.39
  117.0 0.1 reshape.36
  117.1 0.1 copy.36
  117.2 0.8 copy.38
  118.1 79.3 %all-gather.6.cloned.1.call-done = bf16[128,256,128]{2,1,0:T(8,128)(2,1)} async-done(((bf16[2,256,128]{2,1,0:T(8,128)(2,1)}), bf16[128,256,128]{2,1,0:T(8,128)(2,1)}) %all-gather.6.cloned.1.call-update) | async-done | bytes 8388624 | tf_op jit(solution)/shard_map/all_gather | solution.py:48
  197.4 13.9 %pad_maximum_fusion.1 = bf16[256,256,128]{2,1,0:T(8,128)(2,1)} fusion(bf16[128,256,128]{2,1,0:T(8,128)(2,1)} %all-gather.6.cloned.1.call-done, bf16[128,256,128]{2,1,0:T(8,128)(2,1)} %all-gather.4.cloned.1.call-done), kind=kLoop, calls=%fused_computation.4 | loop fusion | flops 8388608 | bytes 33554432 | tf_op jit(solution)/shard_map/concatenate | solution.py:33
  211.3 6.5 %gather_fusion.1 = bf16[16,256,128]{2,1,0:T(8,128)(2,1)S(1)} fusion(bf16[256,256,128]{2,1,0:T(8,128)(2,1)} %pad_maximum_fusion.1, s32[1024]{0:T(1024)S(1)} %pad_clamp_fusion.1), kind=kCustom, calls=%fused_computation.1 | custom fusion | bytes 2097216 | tf_op jit(solution)/shard_map/jit(_take)/gather | solution.py:34
  217.8 0.5 copy.37
  218.4 3.3 fusion.42
  221.7 0.1 reshape.44
  221.8 0.1 copy.40
  221.9 0.8 copy.42
  222.7 79.4 %all-gather.8.cloned.1.call-done = bf16[128,256,128]{2,1,0:T(8,128)(2,1)} async-done(((bf16[2,256,128]{2,1,0:T(8,128)(2,1)}), bf16[128,256,128]{2,1,0:T(8,128)(2,1)}) %all-gather.8.cloned.1.call-update) | async-done | bytes 8388624 | tf_op jit(solution)/shard_map/all_gather | solution.py:48
  302.1 17.7 %pad_maximum_fusion = bf16[384,256,128]{2,1,0:T(8,128)(2,1)} fusion(bf16[128,256,128]{2,1,0:T(8,128)(2,1)} %all-gather.8.cloned.1.call-done, bf16[128,256,128]{2,1,0:T(8,128)(2,1)} %all-gather.6.cloned.1.call-done, bf16[128,256,128]{2,1,0:T(8,128)(2,1)} %all-gather.4.cloned.1.call-done), kind=kLoop, calls=%fused_computation.3 | loop fusion | flops 25165824 | bytes 50331648 | tf_op jit(solution)/shard_map/concatenate | solution.py:33
  319.9 9.0 %gather_fusion.2 = bf16[16,256,128]{2,1,0:T(8,128)(2,1)S(1)} fusion(bf16[384,256,128]{2,1,0:T(8,128)(2,1)} %pad_maximum_fusion, s32[1024]{0:T(1024)S(1)} %pad_clamp_fusion), kind=kCustom, calls=%fused_computation.2 | custom fusion | bytes 2097216 | tf_op jit(solution)/shard_map/jit(_take)/gather | solution.py:34
  328.8 0.5 copy.41
  329.4 2.6 fusion.45
  332.0 0.9 pad_maximum_fusion.2
  (18 shorter events, 0.2 us)
Async XLA Ops:
  6.5 102.5 %all-gather.4.cloned.1.call-start = ((), (), s32[]{:S(2)}) async-start(), calls=%async_computation.1 | async-start | bytes 8519680 | tf_op jit(solution)/shard_map/all_gather | solution.py:48
  23.0 174.4 %all-gather.6.cloned.1.call-start = ((), (), s32[]{:S(2)}) async-start(), calls=%async_computation.2 | async-start | bytes 8519680 | tf_op jit(solution)/shard_map/all_gather | solution.py:48
  117.0 185.2 %all-gather.8.cloned.1.call-start = ((), (), s32[]{:S(2)}) async-start(), calls=%async_computation.3 | async-start | bytes 8519680 | tf_op jit(solution)/shard_map/all_gather | solution.py:48
  118.1 100.3 %copy-start.3 = (bf16[8,256,256]{2,1,0:T(8,128)(2,1)S(1)}, bf16[8,256,256]{2,1,0:T(8,128)(2,1)}, u32[]{:S(2)}) copy-start(bf16[8,256,256]{2,1,0:T(8,128)(2,1)} %param.7) | copy-start | bytes 3145732
  319.8 12.2 %copy-start = (bf16[2,256,128]{2,1,0:T(8,128)(2,1)S(1)}, bf16[2,256,128]{2,1,0:T(8,128)(2,1)}, u32[]{:S(2)}) copy-start(bf16[2,256,128]{2,1,0:T(8,128)(2,1)} %convolution_convert_fusion) | copy-start | bytes 393220
  319.9 12.2 %copy-start.1 = (bf16[2,256,128]{2,1,0:T(8,128)(2,1)S(1)}, bf16[2,256,128]{2,1,0:T(8,128)(2,1)}, u32[]{:S(2)}) copy-start(bf16[2,256,128]{2,1,0:T(8,128)(2,1)} %fusion.39) | copy-start | bytes 393220
  319.9 12.2 %copy-start.2 = (bf16[2,256,128]{2,1,0:T(8,128)(2,1)S(1)}, bf16[2,256,128]{2,1,0:T(8,128)(2,1)}, u32[]{:S(2)}) copy-start(bf16[2,256,128]{2,1,0:T(8,128)(2,1)} %fusion.42) | copy-start | bytes 393220
Sparse Core Ops, SparseCore 0:
  23.1 85.8 all-gather.3
  117.1 80.2 all-gather.5
  221.8 80.2 all-gather.7
where the time goes:
time: 340 us; the launch traced here: 339 us
  waiting for transfers between devices  243 us (71%)
  other arithmetic  34 us (10%)
  local copies, waits for them, and re-layouts  25 us (7%)
  between operations  13.3 us (4%)
  blocking collectives  13.2 us (4%)
  matrix products  11 us (3%)
    all_gather x3, waiting for transfers between devices, shards(): incoming = lax.all_gather(solved, 'rows', axis=0, tiled=True)  243 us
    concatenate x2, other arithmetic, shards(): available = jnp.concatenate(gathered_all, axis=0)  31.6 us
    gather x6, local copies, waits for them, and re-layouts, shards(): picked = jnp.take(available, flat_index[lower:upper], axis=0, mode='clip')  21.2 us
    all_to_all x1, blocking collectives, shards(): lax.all_to_all(kernel_rows, 'rhs', split_axis=1, concat_axis=0, tiled=True)  13.2 us
    dot_general x4, matrix products, shards(): jnp.einsum('bij,bjr->bir', diag_inverse[lower:upper], residual, preferred...  11 us
  transfers between devices with their start and end apart: 3, of which 3 were waited for; matrix products, arithmetic and copies ran while one was open for 1% of the time, Pallas kernels for 0%

commit v1 on v0

--- a/solution.py
+++ b/solution.py
@@ -45,7 +45,9 @@
         ).astype(jnp.bfloat16)
         solved_all.append(solved)
         if level_now + 1 < LEV:
-            incoming = lax.all_gather(solved, "rows", axis=0, tiled=True)
+            incoming = jnp.concatenate(
+                lax.all_to_all(jnp.stack(lax.axis_size("rows") * [solved]), "rows", 0, 0), axis=0
+            )
             gathered_all.append(incoming)
     return jnp.concatenate(solved_all, axis=0).reshape(per_device * block, width)
 

time: 340 us -> 677 us (1.99)
  waiting for transfers between devices: 243 us -> 556 us
  starting transfers between devices: 0.09 us -> 26.1 us
  local copies, waits for them, and re-layouts: 25 us -> 39.5 us
  between operations: 13.3 us -> 0.2 us
    all_to_all x0 -> x3, waiting for transfers between devices: none -> 556 us  [shards(): lax.all_to_all(jnp.stack(lax.axis_size('rows') * [solved]), 'rows', 0, 0)]
    all_gather x3 -> x0, waiting for transfers between devices: 243 us -> none  [shards(): incoming = lax.all_gather(solved, 'rows', axis=0, tiled=True)]
    all_to_all x0 -> x3, starting transfers between devices: none -> 26.1 us  [shards(): lax.all_to_all(jnp.stack(lax.axis_size('rows') * [solved]), 'rows', 0, 0)]
    another operation x0 -> x3, local copies, waits for them, and re-layouts: none -> 15.9 us  [shards(): jnp.stack(lax.axis_size('rows') * [solved])]
  transfers between devices with their start and end apart: 3 -> 3, of which waited for: 3 -> 3; matrix products, arithmetic and copies ran while one was open for 1% -> 0% of each run, Pallas kernels for 0% -> 0%
where the time goes in v1:
time: 677 us
  waiting for transfers between devices  556 us (82%)
  local copies, waits for them, and re-layouts  39.5 us (6%)
  other arithmetic  32.7 us (5%)
  starting transfers between devices  26.1 us (4%)
  blocking collectives  13.2 us (2%)
  matrix products  9.03 us (1%)
    all_to_all x3, waiting for transfers between devices, shards(): lax.all_to_all(jnp.stack(lax.axis_size('rows') * [solved]), 'rows', 0, 0)  556 us
    concatenate x2, other arithmetic, shards(): available = jnp.concatenate(gathered_all, axis=0)  31.6 us
    all_to_all x3, starting transfers between devices, shards(): lax.all_to_all(jnp.stack(lax.axis_size('rows') * [solved]), 'rows', 0, 0)  26.1 us
    gather x6, local copies, waits for them, and re-layouts, shards(): picked = jnp.take(available, flat_index[lower:upper], axis=0, mode='clip')  21.1 us
    another operation x3, local copies, waits for them, and re-layouts, shards(): jnp.stack(lax.axis_size('rows') * [solved])  15.9 us
  transfers between devices with their start and end apart: 3, of which 3 were waited for; matrix products, arithmetic and copies ran while one was open for 0% of the time, Pallas kernels for 0%

profile of v1, /device:TPU:1, one launch (start us, length us, event | category | flops | bytes accessed | tf_op | source)
XLA Modules:
  0.0 676.7 jit_solution(8379123917047182387)
XLA Ops:
  0.0 1.3 copy.27
  1.3 13.2 %all_to_all.31 = bf16[512,4,128]{0,2,1:T(8,128)(2,1)S(1)} all-to-all(bf16[512,4,128]{0,2,1:T(8,128)(2,1)S(1)} %bitcast.63), channel_id=1, replica_groups=mesh['rows'=64,'rhs'=4] {'rhs'}, dimensions={1} | all-to-all | bytes 1048576 | tf_op jit(solution)/shard_map/all_to_all | solution.py:10
  14.5 0.1 copy.28
  14.6 1.2 convolution_convert_fusion
  15.8 5.3 stack.6
  21.1 13.9 %all-to-all-start.1 = ((bf16[64,2,256,128]{3,2,1,0:T(8,128)(2,1)}), bf16[64,2,256,128]{3,2,1,0:T(8,128)(2,1)}, u32[]{:S(2)}, u32[]{:S(2)}) async-start(bf16[64,2,256,128]{3,2,1,0:T(8,128)(2,1)} %stack.6), calls=%async_computation.1 | async-start | bytes 16777216 | tf_op jit(solution)/shard_map/all_to_all | solution.py:49
  35.1 0.1 reshape.46
  35.2 0.1 copy.29
  35.4 0.1 copy.31
  35.5 185.3 %all-to-all-done.1 = bf16[64,2,256,128]{3,2,1,0:T(8,128)(2,1)} async-done(((bf16[64,2,256,128]{3,2,1,0:T(8,128)(2,1)}), bf16[64,2,256,128]{3,2,1,0:T(8,128)(2,1)}, u32[]{:S(2)}, u32[]{:S(2)}) %all-to-all-start.1) | async-done | bytes 8388640 | tf_op jit(solution)/shard_map/all_to_all | solution.py:49
  220.8 4.1 gather_fusion
  224.9 0.5 copy.30
  225.5 2.6 fusion.39
  228.1 5.3 stack.7
  233.4 6.1 all-to-all-start.2
  239.6 0.1 copy.33
  239.7 0.1 copy.35
  239.9 185.4 %all-to-all-done.2 = bf16[64,2,256,128]{3,2,1,0:T(8,128)(2,1)} async-done(((bf16[64,2,256,128]{3,2,1,0:T(8,128)(2,1)}), bf16[64,2,256,128]{3,2,1,0:T(8,128)(2,1)}, u32[]{:S(2)}, u32[]{:S(2)}) %all-to-all-start.2) | async-done | bytes 8388640 | tf_op jit(solution)/shard_map/all_to_all | solution.py:49
  425.3 13.9 %pad_maximum_fusion.1 = bf16[256,256,128]{2,1,0:T(8,128)(2,1)} fusion(bf16[128,256,128]{2,1,0:T(8,128)(2,1)} %bitcast.11, bf16[128,256,128]{2,1,0:T(8,128)(2,1)} %bitcast.4), kind=kLoop, calls=%fused_computation.4 | loop fusion | flops 8388608 | bytes 33554432 | tf_op jit(solution)/shard_map/concatenate | solution.py:33
  439.2 6.5 gather_fusion.1
  445.7 0.5 copy.34
  446.3 2.6 fusion.42
  448.9 5.3 stack.8
  454.2 6.1 all-to-all-start.3
  460.4 0.1 copy.37
  460.5 0.1 copy.39
  460.6 185.4 %all-to-all-done.3 = bf16[64,2,256,128]{3,2,1,0:T(8,128)(2,1)} async-done(((bf16[64,2,256,128]{3,2,1,0:T(8,128)(2,1)}), bf16[64,2,256,128]{3,2,1,0:T(8,128)(2,1)}, u32[]{:S(2)}, u32[]{:S(2)}) %all-to-all-start.3) | async-done | bytes 8388640 | tf_op jit(solution)/shard_map/all_to_all | solution.py:49
  646.1 17.7 %pad_maximum_fusion = bf16[384,256,128]{2,1,0:T(8,128)(2,1)} fusion(bf16[128,256,128]{2,1,0:T(8,128)(2,1)} %bitcast.18, bf16[128,256,128]{2,1,0:T(8,128)(2,1)} %bitcast.11, bf16[128,256,128]{2,1,0:T(8,128)(2,1)} %bitcast.4), kind=kLoop, calls=%fused_computation.3 | loop fusion | flops 25165824 | bytes 50331648 | tf_op jit(solution)/shard_map/concatenate | solution.py:33
  663.8 8.9 %gather_fusion.2 = bf16[16,256,128]{2,1,0:T(8,128)(2,1)S(1)} fusion(bf16[384,256,128]{2,1,0:T(8,128)(2,1)} %pad_maximum_fusion, s32[1024]{0:T(1024)S(1)} %pad_clamp_fusion), kind=kCustom, calls=%fused_computation.2 | custom fusion | bytes 2097216 | tf_op jit(solution)/shard_map/jit(_take)/gather | solution.py:34
  672.7 0.5 copy.38
  673.2 2.6 fusion.45
  675.8 0.9 pad_maximum_fusion.2
  (14 shorter events, 0.4 us)
Async XLA Ops:
  21.1 13.9 %copy-start = (s32[8,8]{1,0:T(8,128)S(1)}, s32[8,8]{1,0:T(8,128)}, u32[]{:S(2)}) copy-start(s32[8,8]{1,0:T(8,128)} %param.8) | copy-start | bytes 772
  21.1 14.0 %copy-start.1 = (s32[8]{0:T(128)S(1)}, s32[8]{0:T(128)}, u32[]{:S(2)}) copy-start(s32[8]{0:T(128)} %param.9) | copy-start | bytes 100
  21.1 199.7 %all-to-all-start.1 = ((bf16[64,2,256,128]{3,2,1,0:T(8,128)(2,1)}), bf16[64,2,256,128]{3,2,1,0:T(8,128)(2,1)}, u32[]{:S(2)}, u32[]{:S(2)}) async-start(bf16[64,2,256,128]{3,2,1,0:T(8,128)(2,1)} %stack.6), calls=%async_computation.1 | async-start | bytes 16777216 | tf_op jit(solution)/shard_map/all_to_all | solution.py:49
  233.4 191.9 %all-to-all-start.2 = ((bf16[64,2,256,128]{3,2,1,0:T(8,128)(2,1)}), bf16[64,2,256,128]{3,2,1,0:T(8,128)(2,1)}, u32[]{:S(2)}, u32[]{:S(2)}) async-start(bf16[64,2,256,128]{3,2,1,0:T(8,128)(2,1)} %stack.7), calls=%async_computation.2 | async-start | bytes 16777216 | tf_op jit(solution)/shard_map/all_to_all | solution.py:49
  454.2 191.9 %all-to-all-start.3 = ((bf16[64,2,256,128]{3,2,1,0:T(8,128)(2,1)}), bf16[64,2,256,128]{3,2,1,0:T(8,128)(2,1)}, u32[]{:S(2)}, u32[]{:S(2)}) async-start(bf16[64,2,256,128]{3,2,1,0:T(8,128)(2,1)} %stack.8), calls=%async_computation.3 | async-start | bytes 16777216 | tf_op jit(solution)/shard_map/all_to_all | solution.py:49
